TPU v7x, 256 devices: a whole 4x4x8 slice. The times are simulated.
256 devices in a mesh: seq: 64 (over y_lo, x, z), fsdp: 4 (over y_hi, core).
Axes of the slice: x: 4, y: 4 (y_hi: 2, y_lo: 2; y = y_hi * 2 + y_lo), z: 8, core: 2. Of those that a mesh axis runs over, the one named last changes fastest.
Arguments:
- inputs: bfloat16 [4, 16384, 1536], P(None, ('seq', 'fsdp')), may hold values from -6 to 6
- cotangent: bfloat16 [4, 16384, 1536], P(None, ('seq', 'fsdp')), may hold values from -24 to 24
- dilated_kernel_weight: bfloat16 [1536, 3, 768], P('seq', None, 'fsdp'), may hold values from -0.09375 to 0.09375
- point_weight: bfloat16 [1536, 768], P('seq', 'fsdp'), may hold values from -0.21875 to 0.21875
Outputs:
- outputs: bfloat16 [4, 16384, 1536], P(None, ('seq', 'fsdp'))
- grad_inputs: bfloat16 [4, 16384, 1536], P(None, ('seq', 'fsdp'))
- grad_conv: float32 [1536, 3, 768], P('seq', None, 'fsdp')
- grad_point: float32 [1536, 768], P('seq', 'fsdp')
All inputs are finite; a program needn't handle non-finite values.
Results may differ from a plain program's by a relative error of at most 0.0053.
Values may be sent and summed in bfloat16 or wider, within the bound.
No kernel may reach another device: no remote copies, remote signals or barrier semaphores. Data moves between devices by JAX's collectives and lax.ppermute only.
A program may use at most 128 MiB of HBM per device.

v0:
```python
import math
import jax
import jax.numpy as jnp
from jax import lax
from jax.sharding import PartitionSpec as P


def shifted(x, axis, by):
    peers = lax.axis_size(axis)
    pairs = [(i, i + by) for i in range(peers) if 0 <= i + by < peers]
    return lax.ppermute(x, axis, pairs)


def gelu_value(v):
    return 0.5 * v * (1.0 + lax.erf(v * (1.0 / math.sqrt(2.0))))


def gelu_slope(v):
    return 0.5 * (1.0 + lax.erf(v * (1.0 / math.sqrt(2.0)))) + v * jnp.exp(-0.5 * v * v) * (
        1.0 / math.sqrt(2.0 * math.pi)
    )


def contract_rows(left, right):
    return lax.dot_general(
        left, right, (((0,), (0,)), ((), ())), preferred_element_type=jnp.float32
    )


def body(inputs, cotangent, dilated_kernel_weight, point_weight):
    seqs, bins, kernel_width = inputs.shape
    rows_all = seqs * bins * lax.axis_size("seq") * lax.axis_size("fsdp")
    norm_factor = 1.0 / math.sqrt(rows_all)
    part_conv, part_point = (
        lax.all_gather(dilated_kernel_weight, "seq", axis=0, tiled=True),
        lax.all_gather(point_weight, "seq", axis=0, tiled=True),
    )
    full_conv, full_point = (
        lax.all_gather(part_conv, "fsdp", axis=2, tiled=True),
        lax.all_gather(part_point, "fsdp", axis=1, tiled=True),
    )
    half_kernel_span = full_point.shape[1]
    x = inputs.astype(jnp.float32)
    scale = lax.rsqrt(jnp.mean(x * x, axis=-1, keepdims=True) + 1e-06)
    normed = x * scale
    input_activations = gelu_value(normed).astype(jnp.bfloat16)
    flat_acts = input_activations.reshape(-1, kernel_width)
    acts_back = shifted(input_activations, ("seq", "fsdp"), 2)
    acts_ahead = shifted(input_activations, ("seq", "fsdp"), -2)
    hidden_state = jnp.dot(flat_acts, full_conv[:, 1, :], preferred_element_type=jnp.float32)
    hidden_state = hidden_state + jnp.dot(
        acts_back.reshape(-1, kernel_width), full_conv[:, 0, :], preferred_element_type=jnp.float32
    )
    hidden_state = hidden_state + jnp.dot(
        acts_ahead.reshape(-1, kernel_width), full_conv[:, 2, :], preferred_element_type=jnp.float32
    )
    mid = gelu_value(hidden_state).astype(jnp.bfloat16)
    mixed = lax.dot_general(
        mid, full_point, (((1,), (1,)), ((), ())), preferred_element_type=jnp.float32
    )
    outputs = (
        (x.reshape(-1, kernel_width) + mixed).astype(jnp.bfloat16).reshape(seqs, bins, kernel_width)
    )
    flat_cot = cotangent.reshape(-1, kernel_width)
    back_mid = jnp.dot(flat_cot, full_point, preferred_element_type=jnp.float32)
    hidden_state_gradient = (
        (back_mid * gelu_slope(hidden_state))
        .astype(jnp.bfloat16)
        .reshape(seqs, bins, half_kernel_span)
    )
    grad_later = shifted(hidden_state_gradient, ("seq", "fsdp"), -2)
    grad_earlier = shifted(hidden_state_gradient, ("seq", "fsdp"), 2)
    stacked_tap_inputs = jnp.concatenate(
        [grad_later, hidden_state_gradient, grad_earlier], axis=-1
    ).reshape(-1, 3 * half_kernel_span)
    grad_acts = lax.dot_general(
        stacked_tap_inputs,
        full_conv.reshape(kernel_width, 3 * half_kernel_span),
        (((1,), (1,)), ((), ())),
        preferred_element_type=jnp.float32,
    )
    grad_normed = grad_acts.reshape(seqs, bins, kernel_width) * gelu_slope(normed)
    inner = jnp.mean(grad_normed * x, axis=-1, keepdims=True)
    grad_inputs = (
        cotangent.astype(jnp.float32) + scale * (grad_normed - x * scale * scale * inner)
    ).astype(jnp.bfloat16)
    conv_part = contract_rows(flat_acts, stacked_tap_inputs)
    point_part = contract_rows(flat_cot, mid)
    summed = lax.psum_scatter(
        jnp.concatenate([conv_part, point_part], axis=1).reshape(
            dilated_kernel_weight.shape[0] * lax.axis_size("seq"), 4, half_kernel_span
        ),
        "seq",
        scatter_dimension=0,
        tiled=True,
    )
    reduced = lax.psum_scatter(summed, "fsdp", scatter_dimension=2, tiled=True)
    grad_conv = reduced[:, 0:3, :] * norm_factor
    grad_point = reduced[:, 3, :] * norm_factor
    return (outputs, grad_inputs, grad_conv, grad_point)


def solution(mesh):
    return jax.shard_map(
        body,
        mesh=mesh,
        in_specs=(
            P(None, ("seq", "fsdp"), None),
            P(None, ("seq", "fsdp"), None),
            P("seq", None, "fsdp"),
            P("seq", "fsdp"),
        ),
        out_specs=(
            P(None, ("seq", "fsdp"), None),
            P(None, ("seq", "fsdp"), None),
            P("seq", None, "fsdp"),
            P("seq", "fsdp"),
        ),
        check_vma=False,
    )
```

profile of v0, /device:TPU:1, one launch (start us, length us, event | category | flops | bytes accessed | tf_op | source)
XLA Modules:
  0.0 964.2 jit_solution(17117318091418794399)
XLA Ops:
  7.2 0.0 all-gather.4.cloned.1.call-start
  7.2 0.7 all-gather.4.cloned.1.call-update
  7.9 0.0 all-gather.6.cloned.1.call-start
  7.9 258.9 %all-gather.4.cloned.1.call-done = bf16[1536,3,192]{2,0,1:T(8,128)(2,1)} async-done(((bf16[24,3,192]{2,0,1:T(8,128)(2,1)}), bf16[1536,3,192]{2,0,1:T(8,128)(2,1)}) %all-gather.4.cloned.1.call-update) | async-done | bytes 1769488 | tf_op jit(solution)/shard_map/all_gather | solution.py:35
  266.8 4.0 copy.20
  270.9 0.0 all-gather.6.cloned.1.call-update
  270.9 0.0 all-gather.8.cloned.1.call-start
  270.9 0.6 copy-done.3
  271.6 132.7 %all_gather.14 = bf16[1536,192]{1,0:T(8,128)(2,1)S(1)} all-gather(bf16[24,192]{1,0:T(8,128)(2,1)S(1)} %copy-done.3), channel_id=1, replica_groups=mesh['seq'=64,'fsdp'=4] {'seq'}, dimensions={0}, use_global_device_ids=true | all-gather | bytes 599040 | tf_op jit(solution)/shard_map/all_gather | solution.py:36
  404.2 1.1 copy.21
  405.3 0.0 all-gather.8.cloned.1.call-update
  405.3 0.0 reduce-scatter.5.cloned.1.call-start
  405.4 0.2 multiply_reduce_fusion.1
  405.6 0.5 multiply_convert_fusion
  406.1 1.3 collective-permute-start.1
  407.4 5.5 collective-permute-start
  412.9 0.0 all-gather.6.cloned.1.call-done
  413.0 2.5 fusion.3
  415.4 5.4 collective-permute-done.1
  420.9 2.5 fusion.1
  423.3 5.7 collective-permute-done
  429.1 0.9 copy-done.2
  429.9 2.8 fusion.9
  432.7 82.0 %all-gather.8.cloned.1.call-done = bf16[1536,768]{0,1:T(8,128)(2,1)} async-done(((bf16[1536,192]{0,1:T(8,128)(2,1)}), bf16[1536,768]{0,1:T(8,128)(2,1)}) %all-gather.8.cloned.1.call-update) | async-done | bytes 2359312 | tf_op jit(solution)/shard_map/all_gather | solution.py:40
  514.7 2.5 fusion.15
  517.3 7.5 collective-permute-start.3
  524.7 1.3 collective-permute-start.2
  526.0 0.9 convolution_bitcast_fusion.1
  526.9 12.2 %collective-permute-done.3 = bf16[4,64,768]{2,1,0:T(8,128)(2,1)S(1)} collective-permute-done((bf16[4,64,768]{2,1,0:T(8,128)(2,1)S(1)}, bf16[4,64,768]{2,1,0:T(8,128)(2,1)S(1)}, u32[]{:S(2)}, u32[]{:S(2)}) %collective-permute-start.3) | collective-permute-done | bytes 393248 | tf_op jit(solution)/shard_map/ppermute | solution.py:11
  539.1 0.7 copy-done.4
  539.9 0.8 copy-done.6
  540.6 7.1 convolution_bitcast_fusion
  547.8 6.6 pad_maximum_fusion
  554.3 7.0 copy.34
  561.3 0.2 reduce-scatter.7.cloned.1.call-start
  561.6 3.4 fusion
  565.0 6.5 multiply_reduce_fusion
  571.5 304.1 %reduce-scatter.5.cloned.1.call-done = f32[24,4,768]{2,0,1:T(8,128)} async-done(((f32[1536,4,768]{2,0,1:T(8,128)}), f32[24,4,768]{2,0,1:T(8,128)}) %reduce-scatter.5.cloned.1.call-update) | async-done | bytes 294928 | tf_op jit(solution)/shard_map/reduce_scatter | solution.py:89
  875.6 1.6 copy.28
  877.2 1.4 reshape.73
  878.7 2.8 add_convert_fusion
  881.5 73.5 %reduce-scatter.7.cloned.1.call-done = f32[192,96]{1,0:T(8,128)} async-done(((f32[768,96]{1,0:T(8,128)}), f32[192,96]{1,0:T(8,128)}) %reduce-scatter.7.cloned.1.call-update) | async-done | bytes 73744
  955.0 1.1 reshape.74
  956.1 0.1 slice.24
  956.2 0.1 copy.30
  956.3 0.7 broadcast_multiply_fusion
  957.0 0.1 copy.31
  957.0 0.6 multiply_bitcast_fusion
  (17 shorter events, 0.1 us)
Async XLA Ops:
  7.2 259.7 %all-gather.4.cloned.1.call-start = ((), (), s32[]{:S(2)}) async-start(), calls=%async_computation.2 | async-start | bytes 2396160 | tf_op jit(solution)/shard_map/all_gather | solution.py:35
  7.9 405.1 %all-gather.6.cloned.1.call-start = ((), (), s32[]{:S(2)}) async-start(), calls=%async_computation.3 | async-start | bytes 8847360 | tf_op jit(solution)/shard_map/all_gather | solution.py:39
  270.9 0.7 copy-start.3
  270.9 134.5 %copy-start = (bf16[4,64,1536]{2,1,0:T(8,128)(2,1)S(1)}, bf16[4,64,1536]{2,1,0:T(8,128)(2,1)}, u32[]{:S(2)}) copy-start(bf16[4,64,1536]{2,1,0:T(8,128)(2,1)} %param.4) | copy-start | bytes 2359300
  270.9 243.8 %all-gather.8.cloned.1.call-start = ((), (), s32[]{:S(2)}) async-start(), calls=%async_computation.4 | async-start | bytes 2949120 | tf_op jit(solution)/shard_map/all_gather | solution.py:40
  405.3 470.3 %reduce-scatter.5.cloned.1.call-start = ((), (), s32[]{:S(2)}) async-start(), calls=%async_computation.5 | async-start | bytes 19169280 | tf_op jit(solution)/shard_map/reduce_scatter | solution.py:89
  406.1 14.8 %collective-permute-start.1 = (bf16[4,64,1536]{2,1,0:T(8,128)(2,1)S(1)}, bf16[4,64,1536]{2,1,0:T(8,128)(2,1)S(1)}, u32[]{:S(2)}, u32[]{:S(2)}) collective-permute-start(bf16[4,64,1536]{2,1,0:T(8,128)(2,1)S(1)} %multiply_convert_fusion), channel_id=1, source_target_pairs={{2,0},{3,1},{4,2},{5,3},{6,4},{7,5},{8,6},{9,7},{10,8},{11,9},{12,... | collective-permute-start | bytes 2359304 | tf_op jit(solution)/shard_map/ppermute | solution.py:11
  407.4 21.7 %collective-permute-start = (bf16[4,64,1536]{2,1,0:T(8,128)(2,1)S(1)}, bf16[4,64,1536]{2,1,0:T(8,128)(2,1)S(1)}, u32[]{:S(2)}, u32[]{:S(2)}) collective-permute-start(bf16[4,64,1536]{2,1,0:T(8,128)(2,1)S(1)} %multiply_convert_fusion), channel_id=1, source_target_pairs={{0,2},{1,3},{2,4},{3,5},{4,6},{5,7},{6,8},{7,9},{8,10},{9,11},{10,... | collective-permute-start | bytes 2359304 | tf_op jit(solution)/shard_map/ppermute | solution.py:11
  429.0 0.9 copy-start.2
  429.9 84.8 %copy-start.1 = (bf16[4,64,1536]{2,1,0:T(8,128)(2,1)S(1)}, bf16[4,64,1536]{2,1,0:T(8,128)(2,1)}, u32[]{:S(2)}) copy-start(bf16[4,64,1536]{2,1,0:T(8,128)(2,1)} %param.5) | copy-start | bytes 2359300
  517.3 21.8 %collective-permute-start.3 = (bf16[4,64,768]{2,1,0:T(8,128)(2,1)S(1)}, bf16[4,64,768]{2,1,0:T(8,128)(2,1)S(1)}, u32[]{:S(2)}, u32[]{:S(2)}) collective-permute-start(bf16[4,64,768]{2,1,0:T(8,128)(2,1)S(1)} %bitcast.59), channel_id=1, source_target_pairs={{0,2},{1,3},{2,4},{3,5},{4,6},{5,7},{6,8},{7,9},{8,10},{9,11},{10,... | collective-permute-start | bytes 1179656 | tf_op jit(solution)/shard_map/ppermute | solution.py:11
  524.7 14.4 %collective-permute-start.2 = (bf16[4,64,768]{2,1,0:T(8,128)(2,1)S(1)}, bf16[4,64,768]{2,1,0:T(8,128)(2,1)S(1)}, u32[]{:S(2)}, u32[]{:S(2)}) collective-permute-start(bf16[4,64,768]{2,1,0:T(8,128)(2,1)S(1)} %bitcast.60), channel_id=1, source_target_pairs={{2,0},{3,1},{4,2},{5,3},{6,4},{7,5},{8,6},{9,7},{10,8},{11,9},{12,... | collective-permute-start | bytes 1179656 | tf_op jit(solution)/shard_map/ppermute | solution.py:11
  539.1 0.7 copy-start.4
  539.9 0.8 copy-start.6
  561.3 393.7 %reduce-scatter.7.cloned.1.call-start = ((), (), s32[]{:S(2)}) async-start(), calls=%async_computation.6 | async-start | bytes 491520
  561.5 3.4 copy-start.5
  561.6 3.4 copy-start.7
Sparse Core Ops, SparseCore 0:
  9.8 257.0 all-gather.3
  271.0 104.6 all-gather.5
  405.4 109.2 all-gather.7
  561.4 314.1 reduce-scatter.4
  878.8 76.1 reduce-scatter.6
where the time goes:
time: 965 us; the launch traced here: 964 us
  waiting for transfers between devices  743 us (77%)
  blocking collectives  133 us (14%)
  matrix products  28.2 us (3%)
  local copies, waits for them, and re-layouts  19.5 us (2%)
  starting transfers between devices  16 us (2%)
  between operations  13.9 us (1%)
  other arithmetic  11.3 us (1%)
    reduce_scatter x1, waiting for transfers between devices, body(): lax.psum_scatter(jnp.concatenate([conv_part, point_part], axis=1).reshape...  304 us
    all_gather x1, waiting for transfers between devices, body(): lax.all_gather(dilated_kernel_weight, 'seq', axis=0, tiled=True)  259 us
    all_gather x1, blocking collectives, body(): lax.all_gather(point_weight, 'seq', axis=0, tiled=True)  133 us
    all_gather x1, waiting for transfers between devices, body(): lax.all_gather(part_point, 'fsdp', axis=1, tiled=True)  82 us
    unnamed x6, waiting for transfers between devices  74.2 us
    ppermute x4, waiting for transfers between devices, shifted(): return lax.ppermute(x, axis, pairs)  23.4 us
  transfers between devices with their start and end apart: 9, of which 7 were waited for; matrix products, arithmetic and copies ran while one was open for 2% of the time, Pallas kernels for 0%

commit v1 on v0

--- a/solution.py
+++ b/solution.py
@@ -33,7 +33,9 @@
     norm_factor = 1.0 / math.sqrt(rows_all)
     part_conv, part_point = (
         lax.all_gather(dilated_kernel_weight, "seq", axis=0, tiled=True),
-        lax.all_gather(point_weight, "seq", axis=0, tiled=True),
+        jnp.concatenate(
+            lax.all_to_all(jnp.stack([point_weight] * lax.axis_size("seq")), "seq", 0, 0), axis=0
+        ),
     )
     full_conv, full_point = (
         lax.all_gather(part_conv, "fsdp", axis=2, tiled=True),

time: 965 us -> 875 us (0.907)
  blocking collectives: 133 us -> 23.1 us
  waiting for transfers between devices: 743 us -> 768 us
    all_gather x1 -> x0, blocking collectives: 133 us -> none  [body(): lax.all_gather(point_weight, 'seq', axis=0, tiled=True)]
    all_gather x1, waiting for transfers between devices: 0.02 us -> 84.8 us  [body(): lax.all_gather(part_conv, 'fsdp', axis=2, tiled=True)]
    all_gather x1, waiting for transfers between devices: 82 us -> 29 us  [body(): lax.all_gather(part_point, 'fsdp', axis=1, tiled=True)]
    all_to_all x0 -> x1, blocking collectives: none -> 23.1 us  [body(): lax.all_to_all(jnp.stack([point_weight] * lax.axis_size('seq')), 'seq', 0...]
  transfers between devices with their start and end apart: 9 -> 9, of which waited for: 7 -> 6; matrix products, arithmetic and copies ran while one was open for 2% -> 3% of each run, Pallas kernels for 0% -> 0%
where the time goes in v1:
time: 875 us; the launch traced here: 874 us
  waiting for transfers between devices  768 us (88%)
  matrix products  28.2 us (3%)
  blocking collectives  23.1 us (3%)
  local copies, waits for them, and re-layouts  19.5 us (2%)
  between operations  14 us (2%)
  other arithmetic  11.3 us (1%)
  starting transfers between devices  10.5 us (1%)
    reduce_scatter x1, waiting for transfers between devices, body(): lax.psum_scatter(jnp.concatenate([conv_part, point_part], axis=1).reshape...  306 us
    all_gather x1, waiting for transfers between devices, body(): lax.all_gather(dilated_kernel_weight, 'seq', axis=0, tiled=True)  259 us
    all_gather x1, waiting for transfers between devices, body(): lax.all_gather(part_conv, 'fsdp', axis=2, tiled=True)  84.8 us
    unnamed x6, waiting for transfers between devices  74.6 us
    all_gather x1, waiting for transfers between devices, body(): lax.all_gather(part_point, 'fsdp', axis=1, tiled=True)  29 us
    all_to_all x1, blocking collectives, body(): lax.all_to_all(jnp.stack([point_weight] * lax.axis_size('seq')), 'seq', 0...  23.1 us
  transfers between devices with their start and end apart: 9, of which 6 were waited for; matrix products, arithmetic and copies ran while one was open for 3% of the time, Pallas kernels for 0%

profile of v1, /device:TPU:1, one launch (start us, length us, event | category | flops | bytes accessed | tf_op | source)
XLA Modules:
  0.0 874.4 jit_solution(5996032466140178739)
XLA Ops:
  7.2 0.0 all-gather.4.cloned.1.call-start
  7.2 0.7 all-gather.4.cloned.1.call-update
  7.9 0.0 all-gather.6.cloned.1.call-start
  7.9 258.9 %all-gather.4.cloned.1.call-done = bf16[1536,3,192]{2,0,1:T(8,128)(2,1)} async-done(((bf16[24,3,192]{2,0,1:T(8,128)(2,1)}), bf16[1536,3,192]{2,0,1:T(8,128)(2,1)}) %all-gather.4.cloned.1.call-update) | async-done | bytes 1769488 | tf_op jit(solution)/shard_map/all_gather | solution.py:35
  266.8 4.0 copy.20
  270.9 0.0 all-gather.6.cloned.1.call-update
  270.9 0.0 all-gather.8.cloned.1.call-start
  270.9 0.6 copy-done.3
  271.6 0.1 stack.2
  271.6 23.1 %all_to_all.5 = bf16[64,24,192]{2,1,0:T(8,128)(2,1)S(1)} all-to-all(bf16[64,24,192]{2,1,0:T(8,128)(2,1)S(1)} %stack.2), channel_id=1, replica_groups=mesh['seq'=64,'fsdp'=4] {'seq'}, dimensions={0} | all-to-all | bytes 1179648 | tf_op jit(solution)/shard_map/all_to_all | solution.py:37
  294.7 1.1 copy.21
  295.8 0.0 all-gather.8.cloned.1.call-update
  295.8 0.0 reduce-scatter.5.cloned.1.call-start
  295.9 0.2 multiply_reduce_fusion.1
  296.1 0.5 multiply_convert_fusion
  296.6 1.3 collective-permute-start.1
  297.9 5.5 collective-permute-start
  303.4 84.8 %all-gather.6.cloned.1.call-done = bf16[1536,3,768]{0,2,1:T(8,128)(2,1)} async-done(((bf16[1536,3,192]{0,2,1:T(8,128)(2,1)}), bf16[1536,3,768]{0,2,1:T(8,128)(2,1)}) %all-gather.6.cloned.1.call-update) | async-done | bytes 7077904 | tf_op jit(solution)/shard_map/all_gather | solution.py:41
  388.2 2.5 fusion.3
  390.7 2.5 fusion.1
  393.2 0.9 copy-done.2
  394.0 2.8 fusion.9
  396.8 29.0 %all-gather.8.cloned.1.call-done = bf16[1536,768]{0,1:T(8,128)(2,1)} async-done(((bf16[1536,192]{0,1:T(8,128)(2,1)}), bf16[1536,768]{0,1:T(8,128)(2,1)}) %all-gather.8.cloned.1.call-update) | async-done | bytes 2359312 | tf_op jit(solution)/shard_map/all_gather | solution.py:42
  425.8 2.5 fusion.15
  428.4 2.0 collective-permute-start.3
  430.4 1.3 collective-permute-start.2
  431.7 0.9 convolution_bitcast_fusion.1
  432.5 14.4 %collective-permute-done.3 = bf16[4,64,768]{2,1,0:T(8,128)(2,1)S(1)} collective-permute-done((bf16[4,64,768]{2,1,0:T(8,128)(2,1)S(1)}, bf16[4,64,768]{2,1,0:T(8,128)(2,1)S(1)}, u32[]{:S(2)}, u32[]{:S(2)}) %collective-permute-start.3) | collective-permute-done | bytes 393248 | tf_op jit(solution)/shard_map/ppermute | solution.py:11
  446.9 0.7 copy-done.4
  447.7 0.8 copy-done.6
  448.4 7.1 convolution_bitcast_fusion
  455.6 6.6 pad_maximum_fusion
  462.1 7.0 copy.34
  469.1 0.0 reduce-scatter.5.cloned.1.call-update
  469.1 0.2 reduce-scatter.7.cloned.1.call-start
  469.4 3.4 fusion
  472.8 6.5 multiply_reduce_fusion
  479.3 306.1 %reduce-scatter.5.cloned.1.call-done = f32[24,4,768]{2,0,1:T(8,128)} async-done(((f32[1536,4,768]{2,0,1:T(8,128)}), f32[24,4,768]{2,0,1:T(8,128)}) %reduce-scatter.5.cloned.1.call-update) | async-done | bytes 294928 | tf_op jit(solution)/shard_map/reduce_scatter | solution.py:91
  785.5 1.6 copy.28
  787.0 1.4 reshape.79
  788.5 2.8 add_convert_fusion
  791.3 73.8 %reduce-scatter.7.cloned.1.call-done = f32[192,96]{1,0:T(8,128)} async-done(((f32[768,96]{1,0:T(8,128)}), f32[192,96]{1,0:T(8,128)}) %reduce-scatter.7.cloned.1.call-update) | async-done | bytes 73744
  865.1 1.1 reshape.80
  866.2 0.1 slice.24
  866.3 0.1 copy.30
  866.5 0.7 broadcast_multiply_fusion
  867.1 0.1 copy.31
  867.2 0.6 multiply_bitcast_fusion
  (18 shorter events, 0.1 us)
Async XLA Ops:
  7.2 259.7 %all-gather.4.cloned.1.call-start = ((), (), s32[]{:S(2)}) async-start(), calls=%async_computation.3 | async-start | bytes 2396160 | tf_op jit(solution)/shard_map/all_gather | solution.py:35
  7.9 380.3 %all-gather.6.cloned.1.call-start = ((), (), s32[]{:S(2)}) async-start(), calls=%async_computation.4 | async-start | bytes 8847360 | tf_op jit(solution)/shard_map/all_gather | solution.py:41
  270.9 0.7 copy-start.3
  270.9 155.0 %all-gather.8.cloned.1.call-start = ((), (), s32[]{:S(2)}) async-start(), calls=%async_computation.5 | async-start | bytes 2949120 | tf_op jit(solution)/shard_map/all_gather | solution.py:42
  271.6 24.3 %copy-start = (bf16[4,64,1536]{2,1,0:T(8,128)(2,1)S(1)}, bf16[4,64,1536]{2,1,0:T(8,128)(2,1)}, u32[]{:S(2)}) copy-start(bf16[4,64,1536]{2,1,0:T(8,128)(2,1)} %param.4) | copy-start | bytes 2359300
  295.8 489.6 %reduce-scatter.5.cloned.1.call-start = ((), (), s32[]{:S(2)}) async-start(), calls=%async_computation.6 | async-start | bytes 19169280 | tf_op jit(solution)/shard_map/reduce_scatter | solution.py:91
  296.6 94.1 %collective-permute-start.1 = (bf16[4,64,1536]{2,1,0:T(8,128)(2,1)S(1)}, bf16[4,64,1536]{2,1,0:T(8,128)(2,1)S(1)}, u32[]{:S(2)}, u32[]{:S(2)}) collective-permute-start(bf16[4,64,1536]{2,1,0:T(8,128)(2,1)S(1)} %multiply_convert_fusion), channel_id=1, source_target_pairs={{2,0},{3,1},{4,2},{5,3},{6,4},{7,5},{8,6},{9,7},{10,8},{11,9},{12,... | collective-permute-start | bytes 2359304 | tf_op jit(solution)/shard_map/ppermute | solution.py:11
  297.9 95.3 %collective-permute-start = (bf16[4,64,1536]{2,1,0:T(8,128)(2,1)S(1)}, bf16[4,64,1536]{2,1,0:T(8,128)(2,1)S(1)}, u32[]{:S(2)}, u32[]{:S(2)}) collective-permute-start(bf16[4,64,1536]{2,1,0:T(8,128)(2,1)S(1)} %multiply_convert_fusion), channel_id=1, source_target_pairs={{0,2},{1,3},{2,4},{3,5},{4,6},{5,7},{6,8},{7,9},{8,10},{9,11},{10,... | collective-permute-start | bytes 2359304 | tf_op jit(solution)/shard_map/ppermute | solution.py:11
  393.2 0.9 copy-start.2
  394.0 31.8 %copy-start.1 = (bf16[4,64,1536]{2,1,0:T(8,128)(2,1)S(1)}, bf16[4,64,1536]{2,1,0:T(8,128)(2,1)}, u32[]{:S(2)}) copy-start(bf16[4,64,1536]{2,1,0:T(8,128)(2,1)} %param.5) | copy-start | bytes 2359300
  428.4 18.5 %collective-permute-start.3 = (bf16[4,64,768]{2,1,0:T(8,128)(2,1)S(1)}, bf16[4,64,768]{2,1,0:T(8,128)(2,1)S(1)}, u32[]{:S(2)}, u32[]{:S(2)}) collective-permute-start(bf16[4,64,768]{2,1,0:T(8,128)(2,1)S(1)} %bitcast.61), channel_id=1, source_target_pairs={{0,2},{1,3},{2,4},{3,5},{4,6},{5,7},{6,8},{7,9},{8,10},{9,11},{10,... | collective-permute-start | bytes 1179656 | tf_op jit(solution)/shard_map/ppermute | solution.py:11
  430.4 16.6 %collective-permute-start.2 = (bf16[4,64,768]{2,1,0:T(8,128)(2,1)S(1)}, bf16[4,64,768]{2,1,0:T(8,128)(2,1)S(1)}, u32[]{:S(2)}, u32[]{:S(2)}) collective-permute-start(bf16[4,64,768]{2,1,0:T(8,128)(2,1)S(1)} %bitcast.62), channel_id=1, source_target_pairs={{2,0},{3,1},{4,2},{5,3},{6,4},{7,5},{8,6},{9,7},{10,8},{11,9},{12,... | collective-permute-start | bytes 1179656 | tf_op jit(solution)/shard_map/ppermute | solution.py:11
  446.9 0.7 copy-start.4
  447.7 0.8 copy-start.6
  469.1 396.0 %reduce-scatter.7.cloned.1.call-start = ((), (), s32[]{:S(2)}) async-start(), calls=%async_computation.7 | async-start | bytes 491520
  469.3 3.4 copy-start.5
  469.4 3.4 copy-start.7
Sparse Core Ops, SparseCore 0:
  9.8 257.0 all-gather.3
  271.0 117.1 all-gather.5
  390.6 35.2 all-gather.7
  469.2 316.1 reduce-scatter.4
  788.6 76.4 reduce-scatter.6
